TPU v7x, 32 devices: a whole 2x2x4 slice. The times are simulated.
32 devices in a mesh: grp: 2 (over x), chan: 16 (over z, y, core).
Axes of the slice: x: 2, y: 2, z: 4, core: 2. Of those that a mesh axis runs over, the one named last changes fastest.
Arguments:
- samples: bfloat16 [128, 62, 8192], P('chan', 'grp'), parts along dimension 1, may hold values from -6 to 6
- eq_gain: float32 [128, 4096], P('chan'), may hold values from 0.5 to 2
- delays: float32 [1024, 64], replicated, may hold values from -64 to 64
Outputs:
- beams: bfloat16 [2, 1024, 4096], P('grp', 'chan'), parts along dimension 0
There are 2 independent parts, one for each index of `grp`. A program takes and returns all parts, laid end to end along the dimension named above; an argument that names none is the same for every part. Nothing has to cross between parts.
All inputs are finite; a program needn't handle non-finite values.
Results may differ from a plain program's by a relative error of at most 0.0034.
Values may be sent and summed in bfloat16 or wider, within the bound.
No kernel may reach another device: no remote copies, remote signals or barrier semaphores. Data moves between devices by JAX's collectives and lax.ppermute only.
A program may use at most 448 MiB of HBM per device.

v0:
```python
import math
import jax
import jax.numpy as jnp
from jax import lax
from jax.sharding import PartitionSpec as P

DISHES = 64
POLS = 2
NB = 1024
TAPS = 16
AVG = 16
SPEC = 16


def pfb_taps(frame_len, tap_count):
    tap_total = tap_count * frame_len
    position = jnp.arange(tap_total, dtype=jnp.float32) + 0.5
    window = 0.5 - 0.5 * jnp.cos(2.0 * math.pi / tap_total * position)
    offset = (position - 0.5 * tap_total) / frame_len
    prototype = window * jnp.sin(math.pi * offset) / (math.pi * offset)
    prototype = prototype / jnp.sqrt(jnp.sum(prototype * prototype))
    return prototype.reshape(tap_count, frame_len)


def cos_sin(numer, denom):
    phase_angle = 2.0 * math.pi / denom * numer.astype(jnp.float32)
    return (jnp.cos(phase_angle), -jnp.sin(phase_angle))


def turn_tables(frame_len):
    outer_len = 2 ** ((frame_len.bit_length() - 1) // 2)
    inner_len = frame_len // outer_len
    half_len = inner_len // 2
    outer_index = jnp.arange(outer_len, dtype=jnp.int32)
    inner_index = jnp.arange(inner_len, dtype=jnp.int32)
    half_index = jnp.arange(half_len, dtype=jnp.int32)
    one_cos, one_sin = cos_sin(outer_index[:, None] * outer_index[None, :] % outer_len, outer_len)
    twist_cos, twist_sin = cos_sin(
        outer_index[:, None] * inner_index[None, :] % frame_len, frame_len
    )
    three_cos, three_sin = cos_sin(
        inner_index[:, None] * half_index[None, :] % inner_len, inner_len
    )
    table_one = jnp.stack([one_cos, one_sin])
    table_three = jnp.stack([three_cos, three_sin])
    return (outer_len, inner_len, table_one, twist_cos, twist_sin, table_three)


def body(samples, eq_gain, delays):
    inputs_here, frame_count, frame_len = samples.shape
    chan_count = frame_len // 2
    groups = lax.axis_size("chan")
    my_index = lax.axis_index("chan")
    chan_here = chan_count // groups
    beams_here = NB // groups
    time_bins = SPEC // AVG
    highest = lax.Precision.HIGHEST
    tap_table = pfb_taps(frame_len, TAPS)
    filtered = jnp.zeros((inputs_here, SPEC, frame_len), jnp.float32)
    for tap_index in range(TAPS):
        filtered = filtered + tap_table[tap_index] * samples[
            :, tap_index : tap_index + SPEC, :
        ].astype(jnp.float32)
    outer_len, inner_len, table_one, twist_cos, twist_sin, table_three = turn_tables(frame_len)
    framed = filtered.reshape(inputs_here, SPEC, outer_len, inner_len)
    section_one = jnp.einsum("rkn,isnm->irskm", table_one, framed, precision=highest)
    real_one = section_one[:, 0]
    imag_one = section_one[:, 1]
    twisted = jnp.stack(
        [real_one * twist_cos - imag_one * twist_sin, real_one * twist_sin + imag_one * twist_cos],
        axis=1,
    )
    section_three = jnp.einsum("irskm,qmj->irqsjk", twisted, table_three, precision=highest)
    spec_real = (section_three[:, 0, 0] - section_three[:, 1, 1]).reshape(
        inputs_here, SPEC, chan_count
    )
    spec_imag = (section_three[:, 0, 1] + section_three[:, 1, 0]).reshape(
        inputs_here, SPEC, chan_count
    )
    gain_row = eq_gain[:, None, :]
    volt_real = (spec_real * gain_row).astype(jnp.bfloat16)
    volt_imag = (spec_imag * gain_row).astype(jnp.bfloat16)
    outgoing = jnp.stack([volt_real, volt_imag], axis=1).transpose(3, 1, 2, 0)
    arrived = lax.all_to_all(outgoing, "chan", split_axis=0, concat_axis=3, tiled=True)
    dish_volts = arrived.reshape(chan_here, 2, SPEC, DISHES, POLS).transpose(0, 1, 4, 2, 3)
    real_part = dish_volts[:, 0]
    imag_part = dish_volts[:, 1]
    volt_operand = jnp.stack(
        [
            jnp.concatenate([real_part, -imag_part], axis=-1),
            jnp.concatenate([imag_part, real_part], axis=-1),
        ],
        axis=1,
    ).reshape(chan_here, 2 * POLS * SPEC, 2 * DISHES)
    low_len = math.gcd(chan_here, 2 ** ((chan_here.bit_length() - 1) // 2))
    high_count = chan_here // low_len
    weight_scale = 1.0 / math.sqrt(DISHES)

    def rotation(channel, scale):
        turns = channel.astype(jnp.float32)[:, None, None] * delays[None, :, :] / frame_len
        turns = turns - jnp.round(turns)
        angle = 2.0 * math.pi * turns
        return (jnp.cos(angle) * scale, -jnp.sin(angle) * scale)

    high_channel = my_index * chan_here + jnp.arange(high_count, dtype=jnp.int32) * low_len
    high_real, high_imag = rotation(high_channel, weight_scale)
    low_real, low_imag = rotation(jnp.arange(low_len, dtype=jnp.int32), 1.0)
    volt_blocks = volt_operand.reshape(high_count, low_len, 2 * POLS * SPEC, 2 * DISHES)

    def one_block(block_args):
        base_real, base_imag, volt_part = block_args
        w_real = (base_real * low_real - base_imag * low_imag).astype(jnp.bfloat16)
        w_imag = (base_real * low_imag + base_imag * low_real).astype(jnp.bfloat16)
        weight_part = jnp.concatenate([w_real, w_imag], axis=-1)
        product = jnp.einsum(
            "cnk,cbk->cnb", volt_part, weight_part, preferred_element_type=jnp.float32
        ).reshape(low_len, 2 * POLS, time_bins, AVG, NB)
        return jnp.sum(product * product, axis=(1, 3)) / AVG

    energy = lax.map(one_block, (high_real, high_imag, volt_blocks))
    power_bins = energy.reshape(chan_here, time_bins, NB).transpose(1, 2, 0).astype(jnp.bfloat16)
    return lax.all_to_all(power_bins, "chan", split_axis=1, concat_axis=2, tiled=True)


def solution(mesh):
    in_specs = (P("chan", "grp", None), P("chan", None), P())
    out_specs = P("grp", "chan", None)
    return jax.shard_map(body, mesh=mesh, in_specs=in_specs, out_specs=out_specs, check_vma=False)
```

profile of v0, /device:TPU:0, one launch (start us, length us, event | category | flops | bytes accessed | tf_op | source)
XLA Modules:
  0.0 574.8 jit_solution(7906501570208651804)
XLA Ops:
  0.0 4.2 fusion.49
  5.4 3.6 fusion.44
  9.0 16.8 %add_bitcast_fusion = f32[8,16,64,128,1]{3,0,2,1,4:T(8,128)S(1)} fusion(bf16[8,31,8192]{2,0,1:T(8,128)(2,1)} %param.5, f32[8192]{0:T(1024)S(1)} %get-tuple-element.151, f32[8192]{0:T(1024)S(1)} %get-tuple-element.152, f32[8192]{0:T(1024)S(1)} %get-tuple-element.153, f32[8192]{0:T(1024)S(1)} %get-tuple-element.154, f32[8192]{0:T(1024)S(1)} %get-tuple-element.155, ...), kind=kLoop, calls=%fused_computation.42 | loop fusion | flops 49283072 | bytes 38273024 | tf_op jit(solution)/shard_map/reshape | solution.py:65
  25.8 7.2 %fusion.33 = f32[8,2,16,64,128]{4,3,1,2,0:T(8,128)S(1)} fusion(f32[8,16,64,128,1]{3,0,2,1,4:T(8,128)S(1)} %add_bitcast_fusion, f32[1,64,64]{2,1,0:T(8,128)S(1)} %get-tuple-element.170, f32[1,64,64]{2,1,0:T(8,128)S(1)} %get-tuple-element.171), kind=kOutput, calls=%fused_computation.43 | convolution fusion | flops 1610620928 | bytes 12615680 | tf_op jit(solution)/shard_map/rkn,isnm->irskm/dot_general | solution.py:66
  33.1 2.0 multiply_subtract_fusion
  35.1 27.7 %fusion.27 = f32[8,2,2,16,64,64]{5,4,3,1,0,2:T(8,128)} fusion(f32[1,128,64]{1,2,0:T(8,128)S(1)} %get-tuple-element.174, f32[1,128,64]{1,2,0:T(8,128)S(1)} %get-tuple-element.175, f32[8,1,16,64,128]{4,3,1,2,0:T(8,128)S(1)} %get-tuple-element.145, f32[8,1,16,64,128]{4,3,1,2,0:T(8,128)S(1)} %get-tuple-element.144), kind=kOutput, calls=%fused_computation.30 | convolution fusion | flops 3223339008 | bytes 16842752 | tf_op jit(solution)/shard_map/irskm,qmj->irqsjk/dot_general | solution.py:73
  62.8 12.1 %slice_subtract_fusion = (f32[8,1,1,16,64,64]{5,4,3,1,0,2:T(8,128)}, f32[8,1,1,16,64,64]{5,4,3,1,0,2:T(8,128)}) fusion(f32[8,2,2,16,64,64]{5,4,3,1,0,2:T(8,128)} %fusion.27), kind=kLoop, calls=%fused_computation.34 | loop fusion | flops 1048576 | bytes 12582912 | tf_op jit(solution)/shard_map/sub | solution.py:74
  74.9 3.5 add.165
  78.4 4.8 sub.47
  83.2 1.9 fusion.37
  85.4 14.0 %copy.57 = bf16[8,2,16,4096]{2,0,1,3:T(8,128)(2,1)} copy(bf16[8,2,16,4096]{3,2,1,0:T(8,128)(2,1)S(1)} %pad_maximum_fusion.2) | data formatting | bytes 4194304 | tf_op jit(solution)/shard_map/stack | solution.py:83
  99.4 14.5 %bitcast_bitcast_fusion = bf16[4096,2,8,16]{3,2,1,0:T(8,128)(2,1)} fusion(bf16[8,2,16,4096]{2,0,1,3:T(8,128)(2,1)} %copy.57), kind=kLoop, calls=%fused_computation.112 | loop fusion | bytes 4194304
  113.9 20.8 %reshape.329 = bf16[16,2,32768]{2,1,0:T(2,128)(2,1)} reshape(bf16[4096,2,8,16]{3,2,1,0:T(8,128)(2,1)} %bitcast_bitcast_fusion) | data formatting | bytes 4194304
  134.7 7.7 %all-to-all-start = ((bf16[16,2,32768]{2,1,0:T(2,128)(2,1)}), bf16[16,2,32768]{2,1,0:T(2,128)(2,1)S(1)}, u32[]{:S(2)}, u32[]{:S(2)}) async-start(bf16[16,2,32768]{2,1,0:T(2,128)(2,1)} %reshape.329), calls=%async_computation | async-start | bytes 4194304 | tf_op jit(solution)/shard_map/all_to_all | solution.py:84
  142.4 17.0 %negate_multiply_fusion = (f32[16,1024,64]{1,2,0:T(8,128)}, f32[16,1024,64]{1,2,0:T(8,128)}) fusion(f32[1024,64]{0,1:T(8,128)S(1)} %copy-done, f32[16]{0:T(128)S(1)} %add_convert_fusion), kind=kLoop, calls=%fused_computation.38 | loop fusion | flops 8388608 | bytes 8650816 | tf_op jit(solution)/shard_map/mul | solution.py:103
  159.4 24.0 %all-to-all-done = bf16[16,2,32768]{2,1,0:T(2,128)(2,1)S(1)} async-done(((bf16[16,2,32768]{2,1,0:T(2,128)(2,1)}), bf16[16,2,32768]{2,1,0:T(2,128)(2,1)S(1)}, u32[]{:S(2)}, u32[]{:S(2)}) %all-to-all-start) | async-done | bytes 2097184 | tf_op jit(solution)/shard_map/all_to_all | solution.py:84
  183.4 14.4 %reshape.330 = bf16[4096,2,8,16]{3,2,1,0:T(8,128)(2,1)} reshape(bf16[16,2,32768]{2,1,0:T(2,128)(2,1)S(1)} %all-to-all-done) | data formatting | bytes 4194304
  197.8 14.6 %copy.59 = bf16[256,2,16,16,8]{0,2,4,3,1:T(8,128)(2,1)S(1)} copy(bf16[256,2,16,16,8]{2,4,1,0,3:T(8,128)(2,1)} %bitcast.87) | data formatting | bytes 4194304 | tf_op jit(solution)/shard_map/all_to_all | solution.py:84
  213.0 2.3 pad_maximum_fusion.1
  215.3 9.0 %copy.60 = bf16[256,2,2,16,128]{4,3,2,1,0:T(8,128)(2,1)} copy(bf16[256,2,2,16,128]{0,3,2,4,1:T(8,128)(2,1)} %pad_maximum_fusion.1) | data formatting | bytes 8388608 | tf_op jit(solution)/shard_map/stack | solution.py:88
  224.3 317.5 %while.12 = (s32[]{:T(128)}, bf16[16,16,1,1024]{3,1,0,2:T(8,128)(2,1)S(1)}, bf16[16,16,64,128]{3,2,1,0:T(8,128)(2,1)}, f32[16,1024,64]{1,2,0:T(8,128)}, f32[16,1...) while((s32[]{:T(128)}, ...), condition=%wide.region_3.4_spmd.clone.clone, body=%wide.region_1.3_spmd.clone.clone.sunk | while | flops 293601280 | bytes 10683037 | solution.py:120
  225.4 17.0 %fusion.84 = (bf16[16,1024,64]{1,2,0:T(8,128)(2,1)S(1)}, bf16[16,1024,64]{1,2,0:T(8,128)(2,1)S(1)}) fusion(f32[1024,64]{0,1:T(8,128)S(1)} %get-tuple-element.248, f32[16]{0:T(128)S(1)} %get-tuple-element.249, f32[1024,64]{0,1:T(8,128)S(1)} %get-tuple-element.223, f32[1024,64]{0,1:T(8,128)S(1)} %get-tuple-element.224), kind=kLoop, calls=%fused_computation.15.clone.1 | loop fusion | flops 14680064 | bytes 4980800 | tf_op jit(solution)/shard_map/while/body/eval_jaxpr/convert_element_type | solution.py:112
  242.4 1.7 multiply_reduce_fusion.2
  245.2 17.0 %fusion.84 = (bf16[16,1024,64]{1,2,0:T(8,128)(2,1)S(1)}, bf16[16,1024,64]{1,2,0:T(8,128)(2,1)S(1)}) fusion(f32[1024,64]{0,1:T(8,128)S(1)} %get-tuple-element.248, f32[16]{0:T(128)S(1)} %get-tuple-element.249, f32[1024,64]{0,1:T(8,128)S(1)} %get-tuple-element.223, f32[1024,64]{0,1:T(8,128)S(1)} %get-tuple-element.224), kind=kLoop, calls=%fused_computation.15.clone.1 | loop fusion | flops 14680064 | bytes 4980800 | tf_op jit(solution)/shard_map/while/body/eval_jaxpr/convert_element_type | solution.py:112
  265.1 17.0 %fusion.84 = (bf16[16,1024,64]{1,2,0:T(8,128)(2,1)S(1)}, bf16[16,1024,64]{1,2,0:T(8,128)(2,1)S(1)}) fusion(f32[1024,64]{0,1:T(8,128)S(1)} %get-tuple-element.248, f32[16]{0:T(128)S(1)} %get-tuple-element.249, f32[1024,64]{0,1:T(8,128)S(1)} %get-tuple-element.223, f32[1024,64]{0,1:T(8,128)S(1)} %get-tuple-element.224), kind=kLoop, calls=%fused_computation.15.clone.1 | loop fusion | flops 14680064 | bytes 4980800 | tf_op jit(solution)/shard_map/while/body/eval_jaxpr/convert_element_type | solution.py:112
  282.1 1.7 multiply_reduce_fusion.2
  284.9 17.0 %fusion.84 = (bf16[16,1024,64]{1,2,0:T(8,128)(2,1)S(1)}, bf16[16,1024,64]{1,2,0:T(8,128)(2,1)S(1)}) fusion(f32[1024,64]{0,1:T(8,128)S(1)} %get-tuple-element.248, f32[16]{0:T(128)S(1)} %get-tuple-element.249, f32[1024,64]{0,1:T(8,128)S(1)} %get-tuple-element.223, f32[1024,64]{0,1:T(8,128)S(1)} %get-tuple-element.224), kind=kLoop, calls=%fused_computation.15.clone.1 | loop fusion | flops 14680064 | bytes 4980800 | tf_op jit(solution)/shard_map/while/body/eval_jaxpr/convert_element_type | solution.py:112
  301.9 1.7 multiply_reduce_fusion.2
  304.8 17.0 %fusion.84 = (bf16[16,1024,64]{1,2,0:T(8,128)(2,1)S(1)}, bf16[16,1024,64]{1,2,0:T(8,128)(2,1)S(1)}) fusion(f32[1024,64]{0,1:T(8,128)S(1)} %get-tuple-element.248, f32[16]{0:T(128)S(1)} %get-tuple-element.249, f32[1024,64]{0,1:T(8,128)S(1)} %get-tuple-element.223, f32[1024,64]{0,1:T(8,128)S(1)} %get-tuple-element.224), kind=kLoop, calls=%fused_computation.15.clone.1 | loop fusion | flops 14680064 | bytes 4980800 | tf_op jit(solution)/shard_map/while/body/eval_jaxpr/convert_element_type | solution.py:112
  324.6 17.0 %fusion.84 = (bf16[16,1024,64]{1,2,0:T(8,128)(2,1)S(1)}, bf16[16,1024,64]{1,2,0:T(8,128)(2,1)S(1)}) fusion(f32[1024,64]{0,1:T(8,128)S(1)} %get-tuple-element.248, f32[16]{0:T(128)S(1)} %get-tuple-element.249, f32[1024,64]{0,1:T(8,128)S(1)} %get-tuple-element.223, f32[1024,64]{0,1:T(8,128)S(1)} %get-tuple-element.224), kind=kLoop, calls=%fused_computation.15.clone.1 | loop fusion | flops 14680064 | bytes 4980800 | tf_op jit(solution)/shard_map/while/body/eval_jaxpr/convert_element_type | solution.py:112
  341.6 1.7 multiply_reduce_fusion.2
  344.5 17.0 %fusion.84 = (bf16[16,1024,64]{1,2,0:T(8,128)(2,1)S(1)}, bf16[16,1024,64]{1,2,0:T(8,128)(2,1)S(1)}) fusion(f32[1024,64]{0,1:T(8,128)S(1)} %get-tuple-element.248, f32[16]{0:T(128)S(1)} %get-tuple-element.249, f32[1024,64]{0,1:T(8,128)S(1)} %get-tuple-element.223, f32[1024,64]{0,1:T(8,128)S(1)} %get-tuple-element.224), kind=kLoop, calls=%fused_computation.15.clone.1 | loop fusion | flops 14680064 | bytes 4980800 | tf_op jit(solution)/shard_map/while/body/eval_jaxpr/convert_element_type | solution.py:112
  361.4 1.7 multiply_reduce_fusion.2
  364.3 17.0 %fusion.84 = (bf16[16,1024,64]{1,2,0:T(8,128)(2,1)S(1)}, bf16[16,1024,64]{1,2,0:T(8,128)(2,1)S(1)}) fusion(f32[1024,64]{0,1:T(8,128)S(1)} %get-tuple-element.248, f32[16]{0:T(128)S(1)} %get-tuple-element.249, f32[1024,64]{0,1:T(8,128)S(1)} %get-tuple-element.223, f32[1024,64]{0,1:T(8,128)S(1)} %get-tuple-element.224), kind=kLoop, calls=%fused_computation.15.clone.1 | loop fusion | flops 14680064 | bytes 4980800 | tf_op jit(solution)/shard_map/while/body/eval_jaxpr/convert_element_type | solution.py:112
  384.1 17.0 %fusion.84 = (bf16[16,1024,64]{1,2,0:T(8,128)(2,1)S(1)}, bf16[16,1024,64]{1,2,0:T(8,128)(2,1)S(1)}) fusion(f32[1024,64]{0,1:T(8,128)S(1)} %get-tuple-element.248, f32[16]{0:T(128)S(1)} %get-tuple-element.249, f32[1024,64]{0,1:T(8,128)S(1)} %get-tuple-element.223, f32[1024,64]{0,1:T(8,128)S(1)} %get-tuple-element.224), kind=kLoop, calls=%fused_computation.15.clone.1 | loop fusion | flops 14680064 | bytes 4980800 | tf_op jit(solution)/shard_map/while/body/eval_jaxpr/convert_element_type | solution.py:112
  401.1 1.7 multiply_reduce_fusion.2
  404.0 17.0 %fusion.84 = (bf16[16,1024,64]{1,2,0:T(8,128)(2,1)S(1)}, bf16[16,1024,64]{1,2,0:T(8,128)(2,1)S(1)}) fusion(f32[1024,64]{0,1:T(8,128)S(1)} %get-tuple-element.248, f32[16]{0:T(128)S(1)} %get-tuple-element.249, f32[1024,64]{0,1:T(8,128)S(1)} %get-tuple-element.223, f32[1024,64]{0,1:T(8,128)S(1)} %get-tuple-element.224), kind=kLoop, calls=%fused_computation.15.clone.1 | loop fusion | flops 14680064 | bytes 4980800 | tf_op jit(solution)/shard_map/while/body/eval_jaxpr/convert_element_type | solution.py:112
  421.0 1.7 multiply_reduce_fusion.2
  423.8 17.0 %fusion.84 = (bf16[16,1024,64]{1,2,0:T(8,128)(2,1)S(1)}, bf16[16,1024,64]{1,2,0:T(8,128)(2,1)S(1)}) fusion(f32[1024,64]{0,1:T(8,128)S(1)} %get-tuple-element.248, f32[16]{0:T(128)S(1)} %get-tuple-element.249, f32[1024,64]{0,1:T(8,128)S(1)} %get-tuple-element.223, f32[1024,64]{0,1:T(8,128)S(1)} %get-tuple-element.224), kind=kLoop, calls=%fused_computation.15.clone.1 | loop fusion | flops 14680064 | bytes 4980800 | tf_op jit(solution)/shard_map/while/body/eval_jaxpr/convert_element_type | solution.py:112
  443.7 17.0 %fusion.84 = (bf16[16,1024,64]{1,2,0:T(8,128)(2,1)S(1)}, bf16[16,1024,64]{1,2,0:T(8,128)(2,1)S(1)}) fusion(f32[1024,64]{0,1:T(8,128)S(1)} %get-tuple-element.248, f32[16]{0:T(128)S(1)} %get-tuple-element.249, f32[1024,64]{0,1:T(8,128)S(1)} %get-tuple-element.223, f32[1024,64]{0,1:T(8,128)S(1)} %get-tuple-element.224), kind=kLoop, calls=%fused_computation.15.clone.1 | loop fusion | flops 14680064 | bytes 4980800 | tf_op jit(solution)/shard_map/while/body/eval_jaxpr/convert_element_type | solution.py:112
  463.5 17.0 %fusion.84 = (bf16[16,1024,64]{1,2,0:T(8,128)(2,1)S(1)}, bf16[16,1024,64]{1,2,0:T(8,128)(2,1)S(1)}) fusion(f32[1024,64]{0,1:T(8,128)S(1)} %get-tuple-element.248, f32[16]{0:T(128)S(1)} %get-tuple-element.249, f32[1024,64]{0,1:T(8,128)S(1)} %get-tuple-element.223, f32[1024,64]{0,1:T(8,128)S(1)} %get-tuple-element.224), kind=kLoop, calls=%fused_computation.15.clone.1 | loop fusion | flops 14680064 | bytes 4980800 | tf_op jit(solution)/shard_map/while/body/eval_jaxpr/convert_element_type | solution.py:112
  480.5 1.7 multiply_reduce_fusion.2
  483.4 17.0 %fusion.84 = (bf16[16,1024,64]{1,2,0:T(8,128)(2,1)S(1)}, bf16[16,1024,64]{1,2,0:T(8,128)(2,1)S(1)}) fusion(f32[1024,64]{0,1:T(8,128)S(1)} %get-tuple-element.248, f32[16]{0:T(128)S(1)} %get-tuple-element.249, f32[1024,64]{0,1:T(8,128)S(1)} %get-tuple-element.223, f32[1024,64]{0,1:T(8,128)S(1)} %get-tuple-element.224), kind=kLoop, calls=%fused_computation.15.clone.1 | loop fusion | flops 14680064 | bytes 4980800 | tf_op jit(solution)/shard_map/while/body/eval_jaxpr/convert_element_type | solution.py:112
  503.2 17.0 %fusion.84 = (bf16[16,1024,64]{1,2,0:T(8,128)(2,1)S(1)}, bf16[16,1024,64]{1,2,0:T(8,128)(2,1)S(1)}) fusion(f32[1024,64]{0,1:T(8,128)S(1)} %get-tuple-element.248, f32[16]{0:T(128)S(1)} %get-tuple-element.249, f32[1024,64]{0,1:T(8,128)S(1)} %get-tuple-element.223, f32[1024,64]{0,1:T(8,128)S(1)} %get-tuple-element.224), kind=kLoop, calls=%fused_computation.15.clone.1 | loop fusion | flops 14680064 | bytes 4980800 | tf_op jit(solution)/shard_map/while/body/eval_jaxpr/convert_element_type | solution.py:112
  523.0 17.0 %fusion.84 = (bf16[16,1024,64]{1,2,0:T(8,128)(2,1)S(1)}, bf16[16,1024,64]{1,2,0:T(8,128)(2,1)S(1)}) fusion(f32[1024,64]{0,1:T(8,128)S(1)} %get-tuple-element.248, f32[16]{0:T(128)S(1)} %get-tuple-element.249, f32[1024,64]{0,1:T(8,128)S(1)} %get-tuple-element.223, f32[1024,64]{0,1:T(8,128)S(1)} %get-tuple-element.224), kind=kLoop, calls=%fused_computation.15.clone.1 | loop fusion | flops 14680064 | bytes 4980800 | tf_op jit(solution)/shard_map/while/body/eval_jaxpr/convert_element_type | solution.py:112
  540.0 1.7 multiply_reduce_fusion.2
  543.4 3.8 reduce.2
  547.4 25.5 %all_to_all.33 = bf16[16,2,8192]{2,1,0:T(2,128)(2,1)S(1)} all-to-all(bf16[16,2,8192]{2,1,0:T(2,128)(2,1)S(1)} %reshape.331), channel_id=1, replica_groups=mesh['grp'=2,'chan'=16] {'chan'}, dimensions={0} | all-to-all | bytes 1048576 | tf_op jit(solution)/shard_map/all_to_all | solution.py:122
  (60 shorter events, 34.0 us)
Async XLA Ops:
  78.4 4.8 copy-start.1
  134.6 7.7 %copy-start = (f32[1024,64]{0,1:T(8,128)S(1)}, f32[1024,64]{0,1:T(8,128)}, u32[]{:S(2)}) copy-start(f32[1024,64]{0,1:T(8,128)} %param.7) | copy-start | bytes 786436
  134.7 48.8 %all-to-all-start = ((bf16[16,2,32768]{2,1,0:T(2,128)(2,1)}), bf16[16,2,32768]{2,1,0:T(2,128)(2,1)S(1)}, u32[]{:S(2)}, u32[]{:S(2)}) async-start(bf16[16,2,32768]{2,1,0:T(2,128)(2,1)} %reshape.329), calls=%async_computation | async-start | bytes 4194304 | tf_op jit(solution)/shard_map/all_to_all | solution.py:84
where the time goes:
time: 584 us; the launch traced here: 575 us
  other arithmetic  337 us (58%)
  local copies, waits for them, and re-layouts  116 us (20%)
  matrix products  62.9 us (11%)
  blocking collectives  25.5 us (4%)
  waiting for transfers between devices  24 us (4%)
  starting transfers between devices  7.66 us (1%)
    convert_element_type x16, other arithmetic, one_block(): w_real = (base_real * low_real - base_imag * low_imag).astype(jnp.bfloat16)  272 us
    unnamed x11, local copies, waits for them, and re-layouts  50.9 us
    dot_general x16, matrix products, one_block(): jnp.einsum('cnk,cbk->cnb', volt_part, weight_part, preferred_element_type...  27.9 us
    dot_general x1, matrix products, body(): jnp.einsum('irskm,qmj->irqsjk', twisted, table_three, precision=highest)  27.7 us
    all_to_all x1, blocking collectives, body(): lax.all_to_all(power_bins, 'chan', split_axis=1, concat_axis=2, tiled=True)  25.5 us
    all_to_all x1, waiting for transfers between devices, body(): lax.all_to_all(outgoing, 'chan', split_axis=0, concat_axis=3, tiled=True)  24 us
    mul x16, local copies, waits for them, and re-layouts, one_block(): w_real = (base_real * low_real - base_imag * low_imag).astype(jnp.bfloat16)  17.1 us
    mul x1, other arithmetic, rotation(): return (jnp.cos(angle) * scale, -jnp.sin(angle) * scale)  17 us
  transfers between devices with their start and end apart: 1, of which 1 were waited for; matrix products, arithmetic and copies ran while one was open for 3% of the time, Pallas kernels for 0%

commit v1 on v0

--- a/solution.py
+++ b/solution.py
@@ -81,7 +81,23 @@
     volt_real = (spec_real * gain_row).astype(jnp.bfloat16)
     volt_imag = (spec_imag * gain_row).astype(jnp.bfloat16)
     outgoing = jnp.stack([volt_real, volt_imag], axis=1).transpose(3, 1, 2, 0)
-    arrived = lax.all_to_all(outgoing, "chan", split_axis=0, concat_axis=3, tiled=True)
+    latest = lax.axis_size("chan")
+    lower = lax.axis_index("chan")
+    v_next, n_now = (latest, lower)
+    out_arr = outgoing.shape[0] // v_next
+    k_now = list(outgoing.shape)
+    k_now[0] = out_arr
+    a_now = k_now[3]
+    k_now[3] = a_now * v_next
+    arrived = jnp.zeros(k_now, outgoing.dtype)
+    for to_i in range(v_next):
+        g_now = lax.dynamic_slice_in_dim(outgoing, (n_now ^ to_i) * out_arr, out_arr, axis=0)
+        if to_i:
+            found = []
+            for c in range(v_next):
+                found.append((c, c ^ to_i))
+            g_now = lax.ppermute(g_now, "chan", found)
+        arrived = lax.dynamic_update_slice_in_dim(arrived, g_now, (n_now ^ to_i) * a_now, axis=3)
     dish_volts = arrived.reshape(chan_here, 2, SPEC, DISHES, POLS).transpose(0, 1, 4, 2, 3)
     real_part = dish_volts[:, 0]
     imag_part = dish_volts[:, 1]

time: 584 us -> 531 us (0.909)
  local copies, waits for them, and re-layouts: 116 us -> 57.2 us
  starting transfers between devices: 7.66 us -> 20 us
    unnamed x11 -> x12, local copies, waits for them, and re-layouts: 50.9 us -> 3 us
    all_to_all x1 -> x0, waiting for transfers between devices: 24 us -> none  [body(): lax.all_to_all(outgoing, 'chan', split_axis=0, concat_axis=3, tiled=True)]
    ppermute x0 -> x15, starting transfers between devices: none -> 20 us  [body(): g_now = lax.ppermute(g_now, 'chan', found)]
    ppermute x0 -> x15, waiting for transfers between devices: none -> 18.7 us  [body(): g_now = lax.ppermute(g_now, 'chan', found)]
    dynamic_update_slice x0 -> x15, local copies, waits for them, and re-layouts: none -> 14.6 us  [body(): lax.dynamic_update_slice_in_dim(arrived, g_now, (n_now ^ to_i) * a_now, a...]
    all_to_all x1 -> x0, local copies, waits for them, and re-layouts: 14.6 us -> none  [body(): lax.all_to_all(outgoing, 'chan', split_axis=0, concat_axis=3, tiled=True)]
    another operation x1 -> x0, local copies, waits for them, and re-layouts: 14 us -> none  [body(): outgoing = jnp.stack([volt_real, volt_imag], axis=1).transpose(3, 1, 2, 0)]
    all_to_all x1 -> x0, starting transfers between devices: 7.66 us -> none  [body(): lax.all_to_all(outgoing, 'chan', split_axis=0, concat_axis=3, tiled=True)]
  transfers between devices with their start and end apart: 1 -> 15, of which waited for: 1 -> 4; matrix products, arithmetic and copies ran while one was open for 3% -> 6% of each run, Pallas kernels for 0% -> 0%
where the time goes in v1:
time: 531 us; the launch traced here: 523 us
  other arithmetic  339 us (64%)
  matrix products  62.9 us (12%)
  local copies, waits for them, and re-layouts  57.2 us (11%)
  blocking collectives  23 us (4%)
  starting transfers between devices  20 us (4%)
  waiting for transfers between devices  18.7 us (4%)
    convert_element_type x16, other arithmetic, one_block(): w_real = (base_real * low_real - base_imag * low_imag).astype(jnp.bfloat16)  272 us
    dot_general x16, matrix products, one_block(): jnp.einsum('cnk,cbk->cnb', volt_part, weight_part, preferred_element_type...  28 us
    dot_general x1, matrix products, body(): jnp.einsum('irskm,qmj->irqsjk', twisted, table_three, precision=highest)  27.7 us
    all_to_all x1, blocking collectives, body(): lax.all_to_all(power_bins, 'chan', split_axis=1, concat_axis=2, tiled=True)  23 us
    ppermute x15, starting transfers between devices, body(): g_now = lax.ppermute(g_now, 'chan', found)  20 us
    ppermute x15, waiting for transfers between devices, body(): g_now = lax.ppermute(g_now, 'chan', found)  18.7 us
    mul x1, other arithmetic, rotation(): return (jnp.cos(angle) * scale, -jnp.sin(angle) * scale)  17.2 us
    mul x16, local copies, waits for them, and re-layouts, one_block(): w_real = (base_real * low_real - base_imag * low_imag).astype(jnp.bfloat16)  17.1 us
  transfers between devices with their start and end apart: 15, of which 4 were waited for; matrix products, arithmetic and copies ran while one was open for 6% of the time, Pallas kernels for 0%

profile of v1, /device:TPU:0, one launch (start us, length us, event | category | flops | bytes accessed | tf_op | source)
XLA Modules:
  0.0 522.7 jit_solution(8344614127759193988)
XLA Ops:
  0.0 4.2 fusion.47
  5.4 3.6 fusion.42
  9.0 16.8 %add_bitcast_fusion = f32[8,16,64,128,1]{3,0,2,1,4:T(8,128)S(1)} fusion(bf16[8,31,8192]{2,0,1:T(8,128)(2,1)} %param.5, f32[8192]{0:T(1024)S(1)} %get-tuple-element.159, f32[8192]{0:T(1024)S(1)} %get-tuple-element.160, f32[8192]{0:T(1024)S(1)} %get-tuple-element.161, f32[8192]{0:T(1024)S(1)} %get-tuple-element.162, f32[8192]{0:T(1024)S(1)} %get-tuple-element.163, ...), kind=kLoop, calls=%fused_computation.74 | loop fusion | flops 49283072 | bytes 38273024 | tf_op jit(solution)/shard_map/reshape | solution.py:65
  25.8 7.2 %fusion.33 = f32[8,2,16,64,128]{4,3,1,2,0:T(8,128)S(1)} fusion(f32[8,16,64,128,1]{3,0,2,1,4:T(8,128)S(1)} %add_bitcast_fusion, f32[1,64,64]{2,1,0:T(8,128)S(1)} %get-tuple-element.178, f32[1,64,64]{2,1,0:T(8,128)S(1)} %get-tuple-element.179), kind=kOutput, calls=%fused_computation.75 | convolution fusion | flops 1610620928 | bytes 12615680 | tf_op jit(solution)/shard_map/rkn,isnm->irskm/dot_general | solution.py:66
  33.1 2.0 multiply_subtract_fusion
  35.1 27.7 %fusion.27 = f32[8,2,2,16,64,64]{5,4,3,1,0,2:T(8,128)} fusion(f32[1,128,64]{1,2,0:T(8,128)S(1)} %get-tuple-element.182, f32[1,128,64]{1,2,0:T(8,128)S(1)} %get-tuple-element.183, f32[8,1,16,64,128]{4,3,1,2,0:T(8,128)S(1)} %get-tuple-element.138, f32[8,1,16,64,128]{4,3,1,2,0:T(8,128)S(1)} %get-tuple-element.137), kind=kOutput, calls=%fused_computation.30 | convolution fusion | flops 3223339008 | bytes 16842752 | tf_op jit(solution)/shard_map/irskm,qmj->irqsjk/dot_general | solution.py:73
  62.8 12.1 %slice_subtract_fusion = (f32[8,1,1,16,64,64]{5,4,3,1,0,2:T(8,128)}, f32[8,1,1,16,64,64]{5,4,3,1,0,2:T(8,128)}) fusion(f32[8,2,2,16,64,64]{5,4,3,1,0,2:T(8,128)} %fusion.27), kind=kLoop, calls=%fused_computation.66 | loop fusion | flops 1048576 | bytes 12582912 | tf_op jit(solution)/shard_map/sub | solution.py:74
  74.9 4.8 add.261
  79.7 4.8 sub.47
  84.4 2.6 multiply_convert_fusion.1
  87.1 4.4 collective-permute-start.10
  96.6 17.2 %negate_multiply_fusion = (f32[16,1024,64]{1,2,0:T(8,128)}, f32[16,1024,64]{1,2,0:T(8,128)}) fusion(f32[1024,64]{0,1:T(8,128)S(1)} %copy-done.2, f32[16]{0:T(128)S(1)} %add_convert_fusion), kind=kLoop, calls=%fused_computation.70 | loop fusion | flops 8388608 | bytes 8650816 | tf_op jit(solution)/shard_map/mul | solution.py:119
  124.4 2.3 collective-permute-start.8
  130.6 2.1 collective-permute-start.11
  133.4 8.4 %collective-permute-done.7 = bf16[256,2,16,8]{0,2,3,1:T(8,128)(2,1)S(1)} collective-permute-done((bf16[256,2,16,8]{0,2,3,1:T(8,128)(2,1)S(1)}, bf16[256,2,16,8]{0,2,3,1:T(8,128)(2,1)S(1)}, u32[]{:S(2)}, u32[]{:S(2)}) %collective-permute-start.7) | collective-permute-done | bytes 131104 | tf_op jit(solution)/shard_map/ppermute | solution.py:99
  145.5 7.5 %collective-permute-done.9 = bf16[256,2,16,8]{0,2,3,1:T(8,128)(2,1)S(1)} collective-permute-done((bf16[256,2,16,8]{0,2,3,1:T(8,128)(2,1)S(1)}, bf16[256,2,16,8]{0,2,3,1:T(8,128)(2,1)S(1)}, u32[]{:S(2)}, u32[]{:S(2)}) %collective-permute-start.9) | collective-permute-done | bytes 131104 | tf_op jit(solution)/shard_map/ppermute | solution.py:99
  158.4 1.8 collective-permute-done.14
  160.8 1.9 slice_bitcast_fusion
  163.5 2.3 pad_maximum_fusion.1
  165.8 9.0 %copy.34 = bf16[256,2,2,16,128]{4,3,2,1,0:T(8,128)(2,1)} copy(bf16[256,2,2,16,128]{0,3,2,4,1:T(8,128)(2,1)} %pad_maximum_fusion.1) | data formatting | bytes 8388608 | tf_op jit(solution)/shard_map/stack | solution.py:104
  174.9 317.5 %while.12 = (s32[]{:T(128)}, bf16[16,16,1,1024]{3,1,0,2:T(8,128)(2,1)S(1)}, bf16[16,16,64,128]{3,2,1,0:T(8,128)(2,1)}, f32[16,1024,64]{1,2,0:T(8,128)}, f32[16,1...) while((s32[]{:T(128)}, ...), condition=%wide.region_3.4_spmd.clone.clone, body=%wide.region_1.3_spmd.clone.clone.sunk | while | flops 293601280 | bytes 10683037 | solution.py:136
  175.9 17.0 %fusion.113 = (bf16[16,1024,64]{1,2,0:T(8,128)(2,1)S(1)}, bf16[16,1024,64]{1,2,0:T(8,128)(2,1)S(1)}) fusion(f32[1024,64]{0,1:T(8,128)S(1)} %get-tuple-element.256, f32[16]{0:T(128)S(1)} %get-tuple-element.257, f32[1024,64]{0,1:T(8,128)S(1)} %get-tuple-element.231, f32[1024,64]{0,1:T(8,128)S(1)} %get-tuple-element.232), kind=kLoop, calls=%fused_computation.15.clone.1 | loop fusion | flops 14680064 | bytes 4980800 | tf_op jit(solution)/shard_map/while/body/eval_jaxpr/convert_element_type | solution.py:128
  192.9 1.7 multiply_reduce_fusion.2
  195.8 17.0 %fusion.113 = (bf16[16,1024,64]{1,2,0:T(8,128)(2,1)S(1)}, bf16[16,1024,64]{1,2,0:T(8,128)(2,1)S(1)}) fusion(f32[1024,64]{0,1:T(8,128)S(1)} %get-tuple-element.256, f32[16]{0:T(128)S(1)} %get-tuple-element.257, f32[1024,64]{0,1:T(8,128)S(1)} %get-tuple-element.231, f32[1024,64]{0,1:T(8,128)S(1)} %get-tuple-element.232), kind=kLoop, calls=%fused_computation.15.clone.1 | loop fusion | flops 14680064 | bytes 4980800 | tf_op jit(solution)/shard_map/while/body/eval_jaxpr/convert_element_type | solution.py:128
  215.6 17.0 %fusion.113 = (bf16[16,1024,64]{1,2,0:T(8,128)(2,1)S(1)}, bf16[16,1024,64]{1,2,0:T(8,128)(2,1)S(1)}) fusion(f32[1024,64]{0,1:T(8,128)S(1)} %get-tuple-element.256, f32[16]{0:T(128)S(1)} %get-tuple-element.257, f32[1024,64]{0,1:T(8,128)S(1)} %get-tuple-element.231, f32[1024,64]{0,1:T(8,128)S(1)} %get-tuple-element.232), kind=kLoop, calls=%fused_computation.15.clone.1 | loop fusion | flops 14680064 | bytes 4980800 | tf_op jit(solution)/shard_map/while/body/eval_jaxpr/convert_element_type | solution.py:128
  232.6 1.7 multiply_reduce_fusion.2
  235.5 17.0 %fusion.113 = (bf16[16,1024,64]{1,2,0:T(8,128)(2,1)S(1)}, bf16[16,1024,64]{1,2,0:T(8,128)(2,1)S(1)}) fusion(f32[1024,64]{0,1:T(8,128)S(1)} %get-tuple-element.256, f32[16]{0:T(128)S(1)} %get-tuple-element.257, f32[1024,64]{0,1:T(8,128)S(1)} %get-tuple-element.231, f32[1024,64]{0,1:T(8,128)S(1)} %get-tuple-element.232), kind=kLoop, calls=%fused_computation.15.clone.1 | loop fusion | flops 14680064 | bytes 4980800 | tf_op jit(solution)/shard_map/while/body/eval_jaxpr/convert_element_type | solution.py:128
  252.4 1.7 multiply_reduce_fusion.2
  255.3 17.0 %fusion.113 = (bf16[16,1024,64]{1,2,0:T(8,128)(2,1)S(1)}, bf16[16,1024,64]{1,2,0:T(8,128)(2,1)S(1)}) fusion(f32[1024,64]{0,1:T(8,128)S(1)} %get-tuple-element.256, f32[16]{0:T(128)S(1)} %get-tuple-element.257, f32[1024,64]{0,1:T(8,128)S(1)} %get-tuple-element.231, f32[1024,64]{0,1:T(8,128)S(1)} %get-tuple-element.232), kind=kLoop, calls=%fused_computation.15.clone.1 | loop fusion | flops 14680064 | bytes 4980800 | tf_op jit(solution)/shard_map/while/body/eval_jaxpr/convert_element_type | solution.py:128
  272.3 1.7 multiply_reduce_fusion.2
  275.1 17.0 %fusion.113 = (bf16[16,1024,64]{1,2,0:T(8,128)(2,1)S(1)}, bf16[16,1024,64]{1,2,0:T(8,128)(2,1)S(1)}) fusion(f32[1024,64]{0,1:T(8,128)S(1)} %get-tuple-element.256, f32[16]{0:T(128)S(1)} %get-tuple-element.257, f32[1024,64]{0,1:T(8,128)S(1)} %get-tuple-element.231, f32[1024,64]{0,1:T(8,128)S(1)} %get-tuple-element.232), kind=kLoop, calls=%fused_computation.15.clone.1 | loop fusion | flops 14680064 | bytes 4980800 | tf_op jit(solution)/shard_map/while/body/eval_jaxpr/convert_element_type | solution.py:128
  295.0 17.0 %fusion.113 = (bf16[16,1024,64]{1,2,0:T(8,128)(2,1)S(1)}, bf16[16,1024,64]{1,2,0:T(8,128)(2,1)S(1)}) fusion(f32[1024,64]{0,1:T(8,128)S(1)} %get-tuple-element.256, f32[16]{0:T(128)S(1)} %get-tuple-element.257, f32[1024,64]{0,1:T(8,128)S(1)} %get-tuple-element.231, f32[1024,64]{0,1:T(8,128)S(1)} %get-tuple-element.232), kind=kLoop, calls=%fused_computation.15.clone.1 | loop fusion | flops 14680064 | bytes 4980800 | tf_op jit(solution)/shard_map/while/body/eval_jaxpr/convert_element_type | solution.py:128
  312.0 1.7 multiply_reduce_fusion.2
  314.8 17.0 %fusion.113 = (bf16[16,1024,64]{1,2,0:T(8,128)(2,1)S(1)}, bf16[16,1024,64]{1,2,0:T(8,128)(2,1)S(1)}) fusion(f32[1024,64]{0,1:T(8,128)S(1)} %get-tuple-element.256, f32[16]{0:T(128)S(1)} %get-tuple-element.257, f32[1024,64]{0,1:T(8,128)S(1)} %get-tuple-element.231, f32[1024,64]{0,1:T(8,128)S(1)} %get-tuple-element.232), kind=kLoop, calls=%fused_computation.15.clone.1 | loop fusion | flops 14680064 | bytes 4980800 | tf_op jit(solution)/shard_map/while/body/eval_jaxpr/convert_element_type | solution.py:128
  334.7 17.0 %fusion.113 = (bf16[16,1024,64]{1,2,0:T(8,128)(2,1)S(1)}, bf16[16,1024,64]{1,2,0:T(8,128)(2,1)S(1)}) fusion(f32[1024,64]{0,1:T(8,128)S(1)} %get-tuple-element.256, f32[16]{0:T(128)S(1)} %get-tuple-element.257, f32[1024,64]{0,1:T(8,128)S(1)} %get-tuple-element.231, f32[1024,64]{0,1:T(8,128)S(1)} %get-tuple-element.232), kind=kLoop, calls=%fused_computation.15.clone.1 | loop fusion | flops 14680064 | bytes 4980800 | tf_op jit(solution)/shard_map/while/body/eval_jaxpr/convert_element_type | solution.py:128
  351.7 1.7 multiply_reduce_fusion.2
  354.5 17.0 %fusion.113 = (bf16[16,1024,64]{1,2,0:T(8,128)(2,1)S(1)}, bf16[16,1024,64]{1,2,0:T(8,128)(2,1)S(1)}) fusion(f32[1024,64]{0,1:T(8,128)S(1)} %get-tuple-element.256, f32[16]{0:T(128)S(1)} %get-tuple-element.257, f32[1024,64]{0,1:T(8,128)S(1)} %get-tuple-element.231, f32[1024,64]{0,1:T(8,128)S(1)} %get-tuple-element.232), kind=kLoop, calls=%fused_computation.15.clone.1 | loop fusion | flops 14680064 | bytes 4980800 | tf_op jit(solution)/shard_map/while/body/eval_jaxpr/convert_element_type | solution.py:128
  374.4 17.0 %fusion.113 = (bf16[16,1024,64]{1,2,0:T(8,128)(2,1)S(1)}, bf16[16,1024,64]{1,2,0:T(8,128)(2,1)S(1)}) fusion(f32[1024,64]{0,1:T(8,128)S(1)} %get-tuple-element.256, f32[16]{0:T(128)S(1)} %get-tuple-element.257, f32[1024,64]{0,1:T(8,128)S(1)} %get-tuple-element.231, f32[1024,64]{0,1:T(8,128)S(1)} %get-tuple-element.232), kind=kLoop, calls=%fused_computation.15.clone.1 | loop fusion | flops 14680064 | bytes 4980800 | tf_op jit(solution)/shard_map/while/body/eval_jaxpr/convert_element_type | solution.py:128
  391.3 1.7 multiply_reduce_fusion.2
  394.2 17.0 %fusion.113 = (bf16[16,1024,64]{1,2,0:T(8,128)(2,1)S(1)}, bf16[16,1024,64]{1,2,0:T(8,128)(2,1)S(1)}) fusion(f32[1024,64]{0,1:T(8,128)S(1)} %get-tuple-element.256, f32[16]{0:T(128)S(1)} %get-tuple-element.257, f32[1024,64]{0,1:T(8,128)S(1)} %get-tuple-element.231, f32[1024,64]{0,1:T(8,128)S(1)} %get-tuple-element.232), kind=kLoop, calls=%fused_computation.15.clone.1 | loop fusion | flops 14680064 | bytes 4980800 | tf_op jit(solution)/shard_map/while/body/eval_jaxpr/convert_element_type | solution.py:128
  414.1 17.0 %fusion.113 = (bf16[16,1024,64]{1,2,0:T(8,128)(2,1)S(1)}, bf16[16,1024,64]{1,2,0:T(8,128)(2,1)S(1)}) fusion(f32[1024,64]{0,1:T(8,128)S(1)} %get-tuple-element.256, f32[16]{0:T(128)S(1)} %get-tuple-element.257, f32[1024,64]{0,1:T(8,128)S(1)} %get-tuple-element.231, f32[1024,64]{0,1:T(8,128)S(1)} %get-tuple-element.232), kind=kLoop, calls=%fused_computation.15.clone.1 | loop fusion | flops 14680064 | bytes 4980800 | tf_op jit(solution)/shard_map/while/body/eval_jaxpr/convert_element_type | solution.py:128
  431.0 1.7 multiply_reduce_fusion.2
  433.9 17.0 %fusion.113 = (bf16[16,1024,64]{1,2,0:T(8,128)(2,1)S(1)}, bf16[16,1024,64]{1,2,0:T(8,128)(2,1)S(1)}) fusion(f32[1024,64]{0,1:T(8,128)S(1)} %get-tuple-element.256, f32[16]{0:T(128)S(1)} %get-tuple-element.257, f32[1024,64]{0,1:T(8,128)S(1)} %get-tuple-element.231, f32[1024,64]{0,1:T(8,128)S(1)} %get-tuple-element.232), kind=kLoop, calls=%fused_computation.15.clone.1 | loop fusion | flops 14680064 | bytes 4980800 | tf_op jit(solution)/shard_map/while/body/eval_jaxpr/convert_element_type | solution.py:128
  453.7 17.0 %fusion.113 = (bf16[16,1024,64]{1,2,0:T(8,128)(2,1)S(1)}, bf16[16,1024,64]{1,2,0:T(8,128)(2,1)S(1)}) fusion(f32[1024,64]{0,1:T(8,128)S(1)} %get-tuple-element.256, f32[16]{0:T(128)S(1)} %get-tuple-element.257, f32[1024,64]{0,1:T(8,128)S(1)} %get-tuple-element.231, f32[1024,64]{0,1:T(8,128)S(1)} %get-tuple-element.232), kind=kLoop, calls=%fused_computation.15.clone.1 | loop fusion | flops 14680064 | bytes 4980800 | tf_op jit(solution)/shard_map/while/body/eval_jaxpr/convert_element_type | solution.py:128
  470.7 1.7 multiply_reduce_fusion.2
  473.6 17.0 %fusion.113 = (bf16[16,1024,64]{1,2,0:T(8,128)(2,1)S(1)}, bf16[16,1024,64]{1,2,0:T(8,128)(2,1)S(1)}) fusion(f32[1024,64]{0,1:T(8,128)S(1)} %get-tuple-element.256, f32[16]{0:T(128)S(1)} %get-tuple-element.257, f32[1024,64]{0,1:T(8,128)S(1)} %get-tuple-element.231, f32[1024,64]{0,1:T(8,128)S(1)} %get-tuple-element.232), kind=kLoop, calls=%fused_computation.15.clone.1 | loop fusion | flops 14680064 | bytes 4980800 | tf_op jit(solution)/shard_map/while/body/eval_jaxpr/convert_element_type | solution.py:128
  494.0 3.8 reduce.2
  497.9 23.0 %all_to_all.18 = bf16[16,2,8192]{2,1,0:T(2,128)(2,1)S(1)} all-to-all(bf16[16,2,8192]{2,1,0:T(2,128)(2,1)S(1)} %reshape.328), channel_id=1, replica_groups=mesh['grp'=2,'chan'=16] {'chan'}, dimensions={0} | all-to-all | bytes 1048576 | tf_op jit(solution)/shard_map/all_to_all | solution.py:138
  (106 shorter events, 64.0 us)
Async XLA Ops:
  79.7 4.8 copy-start.3
  87.1 9.6 %copy-start.2 = (f32[1024,64]{0,1:T(8,128)S(1)}, f32[1024,64]{0,1:T(8,128)}, u32[]{:S(2)}) copy-start(f32[1024,64]{0,1:T(8,128)} %param.7) | copy-start | bytes 786436
  87.1 67.6 %collective-permute-start.10 = (bf16[256,2,16,8]{0,2,3,1:T(8,128)(2,1)S(1)}, bf16[256,2,16,8]{0,2,3,1:T(8,128)(2,1)}, u32[]{:S(2)}, u32[]{:S(2)}) collective-permute-start(bf16[256,2,16,8]{0,2,3,1:T(8,128)(2,1)S(1)} %get-tuple-element.154), channel_id=1, source_target_pairs={{0,11},{1,10},{2,9},{3,8},{4,15},{5,14},{6,13},{7,12},{8,3},{9,2},... | collective-permute-start | bytes 393224 | tf_op jit(solution)/shard_map/ppermute | solution.py:99
  92.3 35.0 %collective-permute-start.5 = (bf16[256,2,16,8]{0,2,3,1:T(8,128)(2,1)}, bf16[256,2,16,8]{0,2,3,1:T(8,128)(2,1)}, u32[]{:S(2)}, u32[]{:S(2)}) collective-permute-start(bf16[256,2,16,8]{0,2,3,1:T(8,128)(2,1)} %get-tuple-element.148), channel_id=1, source_target_pairs={{0,6},{1,7},{2,4},{3,5},{4,2},{5,3},{6,0},{7,1},{8,14},{9,15},{10,... | collective-permute-start | bytes 393224 | tf_op jit(solution)/shard_map/ppermute | solution.py:99
  94.7 20.8 %collective-permute-start = (bf16[256,2,16,8]{0,2,3,1:T(8,128)(2,1)}, bf16[256,2,16,8]{0,2,3,1:T(8,128)(2,1)}, u32[]{:S(2)}, u32[]{:S(2)}) collective-permute-start(bf16[256,2,16,8]{0,2,3,1:T(8,128)(2,1)} %get-tuple-element.142), channel_id=1, source_target_pairs={{0,1},{1,0},{2,3},{3,2},{4,5},{5,4},{6,7},{7,6},{8,9},{9,8},{10,11... | collective-permute-start | bytes 393224 | tf_op jit(solution)/shard_map/ppermute | solution.py:99
  95.1 22.4 %collective-permute-start.1 = (bf16[256,2,16,8]{0,2,3,1:T(8,128)(2,1)}, bf16[256,2,16,8]{0,2,3,1:T(8,128)(2,1)}, u32[]{:S(2)}, u32[]{:S(2)}) collective-permute-start(bf16[256,2,16,8]{0,2,3,1:T(8,128)(2,1)} %get-tuple-element.143), channel_id=1, source_target_pairs={{0,2},{1,3},{2,0},{3,1},{4,6},{5,7},{6,4},{7,5},{8,10},{9,11},{10,... | collective-permute-start | bytes 393224 | tf_op jit(solution)/shard_map/ppermute | solution.py:99
  96.6 24.0 %collective-permute-start.2 = (bf16[256,2,16,8]{0,2,3,1:T(8,128)(2,1)}, bf16[256,2,16,8]{0,2,3,1:T(8,128)(2,1)}, u32[]{:S(2)}, u32[]{:S(2)}) collective-permute-start(bf16[256,2,16,8]{0,2,3,1:T(8,128)(2,1)} %get-tuple-element.144), channel_id=1, source_target_pairs={{0,3},{1,2},{2,1},{3,0},{4,7},{5,6},{6,5},{7,4},{8,11},{9,10},{10,... | collective-permute-start | bytes 393224 | tf_op jit(solution)/shard_map/ppermute | solution.py:99
  114.0 1.4 copy-start
  115.4 7.8 %collective-permute-start.3 = (bf16[256,2,16,8]{0,2,3,1:T(8,128)(2,1)}, bf16[256,2,16,8]{0,2,3,1:T(8,128)(2,1)S(1)}, u32[]{:S(2)}, u32[]{:S(2)}) collective-permute-start(bf16[256,2,16,8]{0,2,3,1:T(8,128)(2,1)} %get-tuple-element.145), channel_id=1, source_target_pairs={{0,4},{1,5},{2,6},{3,7},{4,0},{5,1},{6,2},{7,3},{8,12},{9,13},{10,... | collective-permute-start | bytes 393224 | tf_op jit(solution)/shard_map/ppermute | solution.py:99
  117.5 6.9 %collective-permute-start.4 = (bf16[256,2,16,8]{0,2,3,1:T(8,128)(2,1)}, bf16[256,2,16,8]{0,2,3,1:T(8,128)(2,1)S(1)}, u32[]{:S(2)}, u32[]{:S(2)}) collective-permute-start(bf16[256,2,16,8]{0,2,3,1:T(8,128)(2,1)} %get-tuple-element.146), channel_id=1, source_target_pairs={{0,5},{1,4},{2,7},{3,6},{4,1},{5,0},{6,3},{7,2},{8,13},{9,12},{10,... | collective-permute-start | bytes 393224 | tf_op jit(solution)/shard_map/ppermute | solution.py:99
  120.6 10.0 %collective-permute-start.6 = (bf16[256,2,16,8]{0,2,3,1:T(8,128)(2,1)S(1)}, bf16[256,2,16,8]{0,2,3,1:T(8,128)(2,1)S(1)}, u32[]{:S(2)}, u32[]{:S(2)}) collective-permute-start(bf16[256,2,16,8]{0,2,3,1:T(8,128)(2,1)S(1)} %get-tuple-element.149), channel_id=1, source_target_pairs={{0,7},{1,6},{2,5},{3,4},{4,3},{5,2},{6,1},{7,0},{8,15},{9,14},{10,... | collective-permute-start | bytes 393224 | tf_op jit(solution)/shard_map/ppermute | solution.py:99
  123.3 18.5 %collective-permute-start.7 = (bf16[256,2,16,8]{0,2,3,1:T(8,128)(2,1)S(1)}, bf16[256,2,16,8]{0,2,3,1:T(8,128)(2,1)S(1)}, u32[]{:S(2)}, u32[]{:S(2)}) collective-permute-start(bf16[256,2,16,8]{0,2,3,1:T(8,128)(2,1)S(1)} %get-tuple-element.150), channel_id=1, source_target_pairs={{0,8},{1,9},{2,10},{3,11},{4,12},{5,13},{6,14},{7,15},{8,0},{9,1},... | collective-permute-start | bytes 393224 | tf_op jit(solution)/shard_map/ppermute | solution.py:99
  124.4 19.2 %collective-permute-start.8 = (bf16[256,2,16,8]{0,2,3,1:T(8,128)(2,1)S(1)}, bf16[256,2,16,8]{0,2,3,1:T(8,128)(2,1)S(1)}, u32[]{:S(2)}, u32[]{:S(2)}) collective-permute-start(bf16[256,2,16,8]{0,2,3,1:T(8,128)(2,1)S(1)} %get-tuple-element.151), channel_id=1, source_target_pairs={{0,9},{1,8},{2,11},{3,10},{4,13},{5,12},{6,15},{7,14},{8,1},{9,0},... | collective-permute-start | bytes 393224 | tf_op jit(solution)/shard_map/ppermute | solution.py:99
  127.3 25.7 %collective-permute-start.9 = (bf16[256,2,16,8]{0,2,3,1:T(8,128)(2,1)S(1)}, bf16[256,2,16,8]{0,2,3,1:T(8,128)(2,1)S(1)}, u32[]{:S(2)}, u32[]{:S(2)}) collective-permute-start(bf16[256,2,16,8]{0,2,3,1:T(8,128)(2,1)S(1)} %get-tuple-element.152), channel_id=1, source_target_pairs={{0,10},{1,11},{2,8},{3,9},{4,14},{5,15},{6,12},{7,13},{8,2},{9,3},... | collective-permute-start | bytes 393224 | tf_op jit(solution)/shard_map/ppermute | solution.py:99
  130.6 25.7 %collective-permute-start.11 = (bf16[256,2,16,8]{0,2,3,1:T(8,128)(2,1)S(1)}, bf16[256,2,16,8]{0,2,3,1:T(8,128)(2,1)S(1)}, u32[]{:S(2)}, u32[]{:S(2)}) collective-permute-start(bf16[256,2,16,8]{0,2,3,1:T(8,128)(2,1)S(1)} %get-tuple-element.155), channel_id=1, source_target_pairs={{0,12},{1,13},{2,14},{3,15},{4,8},{5,9},{6,10},{7,11},{8,4},{9,5},... | collective-permute-start | bytes 393224 | tf_op jit(solution)/shard_map/ppermute | solution.py:99
  141.8 15.2 %collective-permute-start.12 = (bf16[256,2,16,8]{0,2,3,1:T(8,128)(2,1)S(1)}, bf16[256,2,16,8]{0,2,3,1:T(8,128)(2,1)S(1)}, u32[]{:S(2)}, u32[]{:S(2)}) collective-permute-start(bf16[256,2,16,8]{0,2,3,1:T(8,128)(2,1)S(1)} %get-tuple-element.153), channel_id=1, source_target_pairs={{0,13},{1,12},{2,15},{3,14},{4,9},{5,8},{6,11},{7,10},{8,5},{9,4},... | collective-permute-start | bytes 393224 | tf_op jit(solution)/shard_map/ppermute | solution.py:99
  143.6 14.1 %collective-permute-start.13 = (bf16[256,2,16,8]{0,2,3,1:T(8,128)(2,1)S(1)}, bf16[256,2,16,8]{0,2,3,1:T(8,128)(2,1)S(1)}, u32[]{:S(2)}, u32[]{:S(2)}) collective-permute-start(bf16[256,2,16,8]{0,2,3,1:T(8,128)(2,1)S(1)} %get-tuple-element.147), channel_id=1, source_target_pairs={{0,14},{1,15},{2,12},{3,13},{4,10},{5,11},{6,8},{7,9},{8,6},{9,7},... | collective-permute-start | bytes 393224 | tf_op jit(solution)/shard_map/ppermute | solution.py:99
  153.0 7.2 %collective-permute-start.14 = (bf16[256,2,16,8]{0,2,3,1:T(8,128)(2,1)S(1)}, bf16[256,2,16,8]{0,2,3,1:T(8,128)(2,1)S(1)}, u32[]{:S(2)}, u32[]{:S(2)}) collective-permute-start(bf16[256,2,16,8]{0,2,3,1:T(8,128)(2,1)S(1)} %get-tuple-element.141), channel_id=1, source_target_pairs={{0,15},{1,14},{2,13},{3,12},{4,11},{5,10},{6,9},{7,8},{8,7},{9,6},... | collective-permute-start | bytes 393224 | tf_op jit(solution)/shard_map/ppermute | solution.py:99
  160.8 2.2 copy-start.1
